TPU v7x, 256 devices: a whole 4x4x8 slice. The times are simulated.
256 devices in a mesh: scene: 16 (over y, z_hi), seq: 16 (over z_lo, x, core).
Axes of the slice: x: 4, y: 4, z: 8 (z_hi: 4, z_lo: 2; z = z_hi * 2 + z_lo), core: 2. Of those that a mesh axis runs over, the one named last changes fastest.
Arguments:
- scene_x: bfloat16 [16, 65536, 256], P('scene', 'seq'), may hold values from -6 to 6
- cotangent: bfloat16 [16, 65536, 256], P('scene', 'seq'), may hold values from -6 to 6
- gate_gain: float32 [256], replicated, may hold values from 0.3 to 3
- kernel: bfloat16 [256, 256, 256], P(None, 'seq'), may hold values from -6 to 6
- block_mix: bfloat16 [256, 256], replicated, may hold values from -0.375 to 0.375
- across_mix: bfloat16 [256, 256], replicated, may hold values from -0.375 to 0.375
- across_unmix: bfloat16 [256, 256], replicated, may hold values from -0.375 to 0.375
- block_unmix: bfloat16 [256, 256], replicated, may hold values from -0.375 to 0.375
Outputs:
- mixed: bfloat16 [16, 65536, 256], P('scene', 'seq')
- grad_x: bfloat16 [16, 65536, 256], P('scene', 'seq')
- grad_kernel: float32 [256, 256, 256], P('scene', 'seq')
- grad_gain: float32 [256], replicated
All inputs are finite; a program needn't handle non-finite values.
Results may differ from a plain program's by a relative error of at most 0.007.
Values may be sent and summed in bfloat16 or wider, within the bound.
No kernel may reach another device: no remote copies, remote signals or barrier semaphores. Data moves between devices by JAX's collectives and lax.ppermute only.
A program may use at most 128 MiB of HBM per device.

v0:
```python
import jax
import jax.numpy as jnp
from jax import lax
from jax.sharding import PartitionSpec as P


def on_device(
    scene_x, cotangent, gate_gain, kernel, block_mix, across_mix, across_unmix, block_unmix
):
    f32 = jnp.float32
    bf16 = jnp.bfloat16
    scenes_here, row_count, channels = scene_x.shape
    block_len = block_mix.shape[0]
    local_a = row_count // block_len
    parts = lax.axis_size("seq")
    chunk = block_len // parts
    kernel_f = kernel.astype(f32)
    inputs = scene_x.reshape(scenes_here, local_a, block_len, channels)
    upstream = cotangent.reshape(scenes_here, local_a, block_len, channels).astype(f32)
    gate_pre = inputs.astype(f32) * gate_gain
    gate_sig = jax.nn.sigmoid(gate_pre)
    gate = gate_pre * gate_sig
    grad_values = (upstream * gate).astype(bf16)
    mix_by_dest = block_mix.reshape(parts, chunk, block_len)
    unmix_by_dest = block_unmix.reshape(block_len, parts, chunk)
    first_mix = jnp.einsum(
        "Jjb,sabc->Jsajc", mix_by_dest, inputs, preferred_element_type=f32
    ).astype(bf16)
    grad_unmixed = jnp.einsum(
        "qJj,saqc->Jsajc", unmix_by_dest, grad_values, preferred_element_type=f32
    ).astype(bf16)
    outgoing = jnp.stack([first_mix, grad_unmixed], axis=1)
    incoming = lax.all_to_all(outgoing, "seq", split_axis=0, concat_axis=0, tiled=True)
    incoming = jnp.moveaxis(incoming, 2, 1)
    spread_mix = incoming[:, :, 0].reshape(parts, scenes_here, local_a, chunk, channels)
    spread_grad = incoming[:, :, 1].reshape(parts, scenes_here, local_a, chunk, channels)
    spread_mix = jnp.moveaxis(spread_mix, 1, 0).reshape(
        scenes_here, parts * local_a, chunk, channels
    )
    spread_grad = jnp.moveaxis(spread_grad, 1, 0).reshape(
        scenes_here, parts * local_a, chunk, channels
    )
    second_mix = jnp.einsum(
        "ia,sajc->sijc", across_mix, spread_mix, preferred_element_type=f32
    ).astype(bf16)
    weighted = (second_mix.astype(f32) * kernel_f).astype(bf16)
    unmixed = jnp.einsum(
        "pi,sijc->spjc", across_unmix, weighted, preferred_element_type=f32
    ).astype(bf16)
    grad_weighted = jnp.einsum(
        "pi,spjc->sijc", across_unmix, spread_grad, preferred_element_type=f32
    )
    kernel_term = jnp.sum(grad_weighted * second_mix.astype(f32), axis=0)
    kernel_grad = lax.psum_scatter(kernel_term, "scene", scatter_dimension=0, tiled=True)
    grad_second = (grad_weighted * kernel_f).astype(bf16)
    grad_first = jnp.einsum(
        "ia,sijc->sajc", across_mix, grad_second, preferred_element_type=f32
    ).astype(bf16)
    back = jnp.stack(
        [
            unmixed.reshape(scenes_here, parts, local_a, chunk, channels),
            grad_first.reshape(scenes_here, parts, local_a, chunk, channels),
        ],
        axis=2,
    )
    back = jnp.moveaxis(back, 1, 0)
    returned = lax.all_to_all(back, "seq", split_axis=0, concat_axis=0, tiled=True)
    values = jnp.einsum(
        "qJj,Jsajc->saqc", unmix_by_dest, returned[:, :, 0], preferred_element_type=f32
    )
    mixed_out = (values * gate).astype(bf16).reshape(scenes_here, row_count, channels)
    grad_gate = upstream * values * gate_sig * (1.0 + gate_pre * (1.0 - gate_sig))
    grad_input = (
        jnp.einsum("Jjb,Jsajc->sabc", mix_by_dest, returned[:, :, 1], preferred_element_type=f32)
        + grad_gate * gate_gain
    )
    grad_input = grad_input.astype(bf16).reshape(scenes_here, row_count, channels)
    gain_term = jnp.sum(inputs.astype(f32) * grad_gate, axis=(0, 1, 2))
    gain_total = lax.psum(gain_term, ("scene", "seq"))
    total_rows = scenes_here * lax.axis_size("scene") * local_a * parts * block_len
    grad_scale = 1.0 / jnp.sqrt(jnp.float32(total_rows))
    return (mixed_out, grad_input, kernel_grad, gain_total * grad_scale)


def solution(mesh):
    return jax.shard_map(
        on_device,
        mesh=mesh,
        in_specs=(
            P("scene", "seq", None),
            P("scene", "seq", None),
            P(),
            P(None, "seq", None),
            P(),
            P(),
            P(),
            P(),
        ),
        out_specs=(P("scene", "seq", None), P("scene", "seq", None), P("scene", "seq", None), P()),
        check_vma=False,
    )
```

profile of v0, /device:TPU:1, one launch (start us, length us, event | category | flops | bytes accessed | tf_op | source)
XLA Modules:
  0.0 296.9 jit_solution(17493549479198899965)
XLA Ops:
  7.2 1.0 copy.33
  8.3 2.5 convert_bitcast_fusion.2
  10.7 0.4 copy-done.7
  11.1 1.4 multiply_convert_fusion
  12.5 0.7 convert_bitcast_fusion.1
  13.2 0.4 pad_maximum_fusion
  13.6 2.5 copy.34
  16.1 7.6 %all-to-all-start = ((bf16[16,2,1,16,16,256]{5,4,3,2,1,0:T(8,128)(2,1)}), bf16[16,2,1,16,16,256]{5,4,3,2,1,0:T(8,128)(2,1)}, u32[]{:S(2)}, u32[]{:S(2)}) async-start(bf16[16,2,1,16,16,256]{5,4,3,2,1,0:T(8,128)(2,1)} %copy.34), calls=%async_computation | async-start | bytes 8388608 | tf_op jit(solution)/shard_map/all_to_all | solution.py:33
  23.7 2.7 copy.37
  26.5 50.9 %all-to-all-done = bf16[16,2,1,16,16,256]{5,4,3,2,1,0:T(8,128)(2,1)} async-done(((bf16[16,2,1,16,16,256]{5,4,3,2,1,0:T(8,128)(2,1)}), bf16[16,2,1,16,16,256]{5,4,3,2,1,0:T(8,128)(2,1)}, u32[]{:S(2)}, u32[]{:S(2)}) %all-to-all-start) | async-done | bytes 4194336 | tf_op jit(solution)/shard_map/all_to_all | solution.py:33
  77.4 2.6 copy.70
  80.0 0.3 fusion.36
  80.3 0.6 copy-done.9
  80.9 1.7 fusion.22
  82.6 1.7 fusion.18
  84.3 0.8 fusion.28
  85.1 1.2 copy-done.1
  86.2 0.8 fusion.25
  87.0 1.2 copy.42
  88.2 1.2 copy.43
  89.4 2.3 maximum_bitcast_fusion
  91.7 12.0 %all-to-all-start.1 = ((bf16[16,1,2,16,16,256]{5,4,3,2,1,0:T(8,128)(2,1)}), bf16[16,1,2,16,16,256]{5,4,3,2,1,0:T(8,128)(2,1)}, u32[]{:S(2)}, u32[]{:S(2)}) async-start(bf16[16,1,2,16,16,256]{5,4,3,2,1,0:T(8,128)(2,1)} %maximum_bitcast_fusion), calls=%async_computation.1 | async-start | bytes 8388608 | tf_op jit(solution)/shard_map/all_to_all | solution.py:67
  103.7 4.6 %fusion.4 = f32[256,16,256]{0,2,1:T(8,128)} fusion(f32[16,256,256]{2,1,0:T(8,128)} %copy-done.1, bf16[16,256,256]{2,1,0:T(8,128)(2,1)S(1)} %fusion.22), kind=kLoop, calls=%fused_computation.10 | loop fusion | flops 2097152 | bytes 10485760 | tf_op jit(solution)/shard_map/reduce_sum | solution.py:53
  108.3 5.5 %copy.46 = f32[256,16,256]{2,1,0:T(8,128)} copy(f32[256,16,256]{0,2,1:T(8,128)} %fusion.4) | data formatting | bytes 8388608 | tf_op jit(solution)/shard_map/reduce_sum | solution.py:53
  113.9 73.7 %all-to-all-done.1 = bf16[16,1,2,16,16,256]{5,4,3,2,1,0:T(8,128)(2,1)} async-done(((bf16[16,1,2,16,16,256]{5,4,3,2,1,0:T(8,128)(2,1)}), bf16[16,1,2,16,16,256]{5,4,3,2,1,0:T(8,128)(2,1)}, u32[]{:S(2)}, u32[]{:S(2)}) %all-to-all-start.1) | async-done | bytes 4194336 | tf_op jit(solution)/shard_map/all_to_all | solution.py:67
  187.6 4.1 %fusion.35 = (bf16[16,1,1,16,16,256]{5,4,3,2,1,0:T(8,128)(2,1)}, bf16[16,1,1,16,16,256]{5,4,3,2,1,0:T(8,128)(2,1)S(1)}) fusion(bf16[16,1,2,16,16,256]{5,4,3,2,1,0:T(8,128)(2,1)} %all-to-all-done.1), kind=kLoop, calls=%fused_computation.44 | loop fusion | bytes 8388608 | tf_op jit(solution)/shard_map/slice | solution.py:74
  191.6 3.6 %fusion.7 = (f32[1,16,256,256]{3,2,1,0:T(8,128)S(1)}, bf16[1,16,256,256]{3,2,1,0:T(8,128)(2,1)}) fusion(f32[256]{0:T(256)S(1)} %copy-done.11, bf16[1,4096,256]{2,1,0:T(8,128)(2,1)S(1)} %copy-done.3, bf16[256,16,16,1]{0,2,1,3:T(8,128)(2,1)S(1)} %bitcast.170, bf16[16,1,1,16,16,256]{5,4,3,2,1,0:T(8,128)(2,1)S(1)} %get-tuple-element.15, ...), kind=kOutput, calls=%fused_computation.15 | convolution fusion | flops 552599552 | bytes 12715008 | tf_op jit(solution)/shard_map/qJj,Jsajc->saqc/dot_general | solution.py:68
  195.3 2.0 copy-done.5
  197.2 0.7 multiply_reduce_fusion
  198.0 86.4 %psum.7 = f32[256]{0:T(256)S(1)} all-reduce(f32[256]{0:T(256)S(1)} %multiply_reduce_fusion), channel_id=1, replica_groups=mesh['scene'=16,'seq'=16] {'scene','seq'}, use_global_device_ids=true, to_apply=%region_2.0 | all-reduce | flops 256 | bytes 2048 | tf_op jit(solution)/shard_map/psum | solution.py:79
  284.4 0.6 broadcast_multiply_fusion
  285.0 5.1 %fusion.2 = bf16[1,16,256,256]{3,2,1,0:T(8,128)(2,1)} fusion(f32[1,16,256,256]{3,2,1,0:T(8,128)} %copy-done.5, bf16[16,16,256,1]{2,1,0,3:T(8,128)(2,1)S(1)} %bitcast.158, bf16[16,1,1,16,16,256]{5,4,3,2,1,0:T(8,128)(2,1)} %get-tuple-element.14, f32[256]{0:T(256)S(1)} %copy-done.11), kind=kOutput, calls=%fused_computation.7 | convolution fusion | flops 540016640 | bytes 8520704 | tf_op jit(solution)/shard_map/Jjb,Jsajc->sabc/dot_general | solution.py:74
  (23 shorter events, 0.1 us)
Async XLA Ops:
  7.2 1.1 copy-start
  8.2 2.5 copy-start.2
  8.2 2.8 copy-start.7
  8.3 2.8 copy-start.11
  16.1 7.6 %copy-start.6 = (bf16[256,16,256]{2,1,0:T(8,128)(2,1)S(1)}, bf16[256,16,256]{2,1,0:T(8,128)(2,1)}, u32[]{:S(2)}) copy-start(bf16[256,16,256]{2,1,0:T(8,128)(2,1)} %param.11) | copy-start | bytes 6291460
  16.1 61.2 %all-to-all-start = ((bf16[16,2,1,16,16,256]{5,4,3,2,1,0:T(8,128)(2,1)}), bf16[16,2,1,16,16,256]{5,4,3,2,1,0:T(8,128)(2,1)}, u32[]{:S(2)}, u32[]{:S(2)}) async-start(bf16[16,2,1,16,16,256]{5,4,3,2,1,0:T(8,128)(2,1)} %copy.34), calls=%async_computation | async-start | bytes 8388608 | tf_op jit(solution)/shard_map/all_to_all | solution.py:33
  80.0 0.9 copy-start.9
  80.9 1.7 copy-start.10
  82.6 1.7 copy-start.4
  84.3 1.9 copy-start.1
  91.7 95.9 %all-to-all-start.1 = ((bf16[16,1,2,16,16,256]{5,4,3,2,1,0:T(8,128)(2,1)}), bf16[16,1,2,16,16,256]{5,4,3,2,1,0:T(8,128)(2,1)}, u32[]{:S(2)}, u32[]{:S(2)}) async-start(bf16[16,1,2,16,16,256]{5,4,3,2,1,0:T(8,128)(2,1)} %maximum_bitcast_fusion), calls=%async_computation.1 | async-start | bytes 8388608 | tf_op jit(solution)/shard_map/all_to_all | solution.py:67
  103.7 186.4 %reduce-scatter.2.cloned.1.call-start = ((), (), s32[]{:S(2)}) async-start(), calls=%async_computation.3 | async-start | bytes 4456448 | tf_op jit(solution)/shard_map/reduce_scatter | solution.py:54
  113.8 77.8 %copy-start.3 = (bf16[1,4096,256]{2,1,0:T(8,128)(2,1)S(1)}, bf16[1,4096,256]{2,1,0:T(8,128)(2,1)}, u32[]{:S(2)}) copy-start(bf16[1,4096,256]{2,1,0:T(8,128)(2,1)} %param.8) | copy-start | bytes 6291460
  187.6 4.1 %copy-start.8 = (bf16[1,4096,256]{2,1,0:T(8,128)(2,1)S(1)}, bf16[1,4096,256]{2,1,0:T(8,128)(2,1)}, u32[]{:S(2)}) copy-start(bf16[1,4096,256]{2,1,0:T(8,128)(2,1)} %param.9) | copy-start | bytes 6291460
  195.3 2.0 copy-start.5
Sparse Core Ops, SparseCore 0:
  114.0 102.4 reduce-scatter.1
where the time goes:
time: 297 us
  waiting for transfers between devices  125 us (42%)
  blocking collectives  86.4 us (29%)
  local copies, waits for them, and re-layouts  25.3 us (9%)
  starting transfers between devices  19.6 us (7%)
  matrix products  16.7 us (6%)
  between operations  14.2 us (5%)
  other arithmetic  9.95 us (3%)
    psum x1, blocking collectives, on_device(): gain_total = lax.psum(gain_term, ('scene', 'seq'))  86.4 us
    all_to_all x1, waiting for transfers between devices, on_device(): lax.all_to_all(back, 'seq', split_axis=0, concat_axis=0, tiled=True)  73.7 us
    all_to_all x1, waiting for transfers between devices, on_device(): lax.all_to_all(outgoing, 'seq', split_axis=0, concat_axis=0, tiled=True)  50.9 us
    all_to_all x1, starting transfers between devices, on_device(): lax.all_to_all(back, 'seq', split_axis=0, concat_axis=0, tiled=True)  12 us
    unnamed x26, local copies, waits for them, and re-layouts  7.9 us
    all_to_all x1, starting transfers between devices, on_device(): lax.all_to_all(outgoing, 'seq', split_axis=0, concat_axis=0, tiled=True)  7.6 us
  transfers between devices with their start and end apart: 3, of which 2 were waited for; matrix products, arithmetic and copies ran while one was open for 9% of the time, Pallas kernels for 0%

commit v1 on v0

--- a/solution.py
+++ b/solution.py
@@ -76,7 +76,7 @@
     )
     grad_input = grad_input.astype(bf16).reshape(scenes_here, row_count, channels)
     gain_term = jnp.sum(inputs.astype(f32) * grad_gate, axis=(0, 1, 2))
-    gain_total = lax.psum(gain_term, ("scene", "seq"))
+    gain_total = jnp.sum(lax.all_gather(gain_term, ("scene", "seq")), axis=0)
     total_rows = scenes_here * lax.axis_size("scene") * local_a * parts * block_len
     grad_scale = 1.0 / jnp.sqrt(jnp.float32(total_rows))
     return (mixed_out, grad_input, kernel_grad, gain_total * grad_scale)

time: 297 us -> 282 us (0.949)
  blocking collectives: 86.4 us -> 71.1 us
    psum x1 -> x0, blocking collectives: 86.4 us -> none  [on_device(): gain_total = lax.psum(gain_term, ('scene', 'seq'))]
    all_gather x0 -> x1, blocking collectives: none -> 71.1 us  [on_device(): gain_total = jnp.sum(lax.all_gather(gain_term, ('scene', 'seq')), axis=0)]
  transfers between devices with their start and end apart: 3 -> 3, of which waited for: 2 -> 2; matrix products, arithmetic and copies ran while one was open for 9% -> 10% of each run, Pallas kernels for 0% -> 0%
where the time goes in v1:
time: 282 us; the launch traced here: 281 us
  waiting for transfers between devices  125 us (44%)
  blocking collectives  71.1 us (25%)
  local copies, waits for them, and re-layouts  24.6 us (9%)
  starting transfers between devices  19.6 us (7%)
  matrix products  16.7 us (6%)
  between operations  14.2 us (5%)
  other arithmetic  10.2 us (4%)
    all_to_all x1, waiting for transfers between devices, on_device(): lax.all_to_all(back, 'seq', split_axis=0, concat_axis=0, tiled=True)  73.7 us
    all_gather x1, blocking collectives, on_device(): gain_total = jnp.sum(lax.all_gather(gain_term, ('scene', 'seq')), axis=0)  71.1 us
    all_to_all x1, waiting for transfers between devices, on_device(): lax.all_to_all(outgoing, 'seq', split_axis=0, concat_axis=0, tiled=True)  50.9 us
    all_to_all x1, starting transfers between devices, on_device(): lax.all_to_all(back, 'seq', split_axis=0, concat_axis=0, tiled=True)  12 us
    all_to_all x1, starting transfers between devices, on_device(): lax.all_to_all(outgoing, 'seq', split_axis=0, concat_axis=0, tiled=True)  7.6 us
    unnamed x26, local copies, waits for them, and re-layouts  7.2 us
  transfers between devices with their start and end apart: 3, of which 2 were waited for; matrix products, arithmetic and copies ran while one was open for 10% of the time, Pallas kernels for 0%

profile of v1, /device:TPU:1, one launch (start us, length us, event | category | flops | bytes accessed | tf_op | source)
XLA Modules:
  0.0 281.2 jit_solution(5366517599819968146)
XLA Ops:
  7.2 1.0 copy.33
  8.3 2.5 convert_bitcast_fusion.2
  10.7 0.4 copy-done.7
  11.1 1.4 multiply_convert_fusion
  12.5 0.7 convert_bitcast_fusion.1
  13.2 0.4 pad_maximum_fusion
  13.6 2.5 copy.34
  16.1 7.6 %all-to-all-start = ((bf16[16,2,1,16,16,256]{5,4,3,2,1,0:T(8,128)(2,1)}), bf16[16,2,1,16,16,256]{5,4,3,2,1,0:T(8,128)(2,1)}, u32[]{:S(2)}, u32[]{:S(2)}) async-start(bf16[16,2,1,16,16,256]{5,4,3,2,1,0:T(8,128)(2,1)} %copy.34), calls=%async_computation | async-start | bytes 8388608 | tf_op jit(solution)/shard_map/all_to_all | solution.py:33
  23.7 2.7 copy.37
  26.5 50.9 %all-to-all-done = bf16[16,2,1,16,16,256]{5,4,3,2,1,0:T(8,128)(2,1)} async-done(((bf16[16,2,1,16,16,256]{5,4,3,2,1,0:T(8,128)(2,1)}), bf16[16,2,1,16,16,256]{5,4,3,2,1,0:T(8,128)(2,1)}, u32[]{:S(2)}, u32[]{:S(2)}) %all-to-all-start) | async-done | bytes 4194336 | tf_op jit(solution)/shard_map/all_to_all | solution.py:33
  77.4 2.6 copy.70
  80.0 0.3 fusion.36
  80.3 0.6 copy-done.9
  80.9 1.7 fusion.22
  82.6 1.7 fusion.18
  84.3 0.8 fusion.28
  85.1 1.2 copy-done.1
  86.2 0.8 fusion.25
  87.0 1.2 copy.42
  88.2 1.2 copy.43
  89.4 2.3 maximum_bitcast_fusion
  91.7 12.0 %all-to-all-start.1 = ((bf16[16,1,2,16,16,256]{5,4,3,2,1,0:T(8,128)(2,1)}), bf16[16,1,2,16,16,256]{5,4,3,2,1,0:T(8,128)(2,1)}, u32[]{:S(2)}, u32[]{:S(2)}) async-start(bf16[16,1,2,16,16,256]{5,4,3,2,1,0:T(8,128)(2,1)} %maximum_bitcast_fusion), calls=%async_computation.1 | async-start | bytes 8388608 | tf_op jit(solution)/shard_map/all_to_all | solution.py:67
  103.7 4.6 %fusion.4 = f32[256,16,256]{0,2,1:T(8,128)} fusion(f32[16,256,256]{2,1,0:T(8,128)} %copy-done.1, bf16[16,256,256]{2,1,0:T(8,128)(2,1)S(1)} %fusion.22), kind=kLoop, calls=%fused_computation.10 | loop fusion | flops 2097152 | bytes 10485760 | tf_op jit(solution)/shard_map/reduce_sum | solution.py:53
  108.3 5.5 %copy.46 = f32[256,16,256]{2,1,0:T(8,128)} copy(f32[256,16,256]{0,2,1:T(8,128)} %fusion.4) | data formatting | bytes 8388608 | tf_op jit(solution)/shard_map/reduce_sum | solution.py:53
  113.9 73.7 %all-to-all-done.1 = bf16[16,1,2,16,16,256]{5,4,3,2,1,0:T(8,128)(2,1)} async-done(((bf16[16,1,2,16,16,256]{5,4,3,2,1,0:T(8,128)(2,1)}), bf16[16,1,2,16,16,256]{5,4,3,2,1,0:T(8,128)(2,1)}, u32[]{:S(2)}, u32[]{:S(2)}) %all-to-all-start.1) | async-done | bytes 4194336 | tf_op jit(solution)/shard_map/all_to_all | solution.py:67
  187.6 4.1 %fusion.35 = (bf16[16,1,1,16,16,256]{5,4,3,2,1,0:T(8,128)(2,1)}, bf16[16,1,1,16,16,256]{5,4,3,2,1,0:T(8,128)(2,1)S(1)}) fusion(bf16[16,1,2,16,16,256]{5,4,3,2,1,0:T(8,128)(2,1)} %all-to-all-done.1), kind=kLoop, calls=%fused_computation.44 | loop fusion | bytes 8388608 | tf_op jit(solution)/shard_map/slice | solution.py:74
  191.6 3.6 %fusion.7 = (f32[1,16,256,256]{3,2,1,0:T(8,128)S(1)}, bf16[1,16,256,256]{3,2,1,0:T(8,128)(2,1)}) fusion(f32[256]{0:T(256)S(1)} %copy-done.11, bf16[1,4096,256]{2,1,0:T(8,128)(2,1)S(1)} %copy-done.3, bf16[256,16,16,1]{0,2,1,3:T(8,128)(2,1)S(1)} %bitcast.171, bf16[16,1,1,16,16,256]{5,4,3,2,1,0:T(8,128)(2,1)S(1)} %get-tuple-element.15, ...), kind=kOutput, calls=%fused_computation.15 | convolution fusion | flops 552599552 | bytes 12715008 | tf_op jit(solution)/shard_map/qJj,Jsajc->saqc/dot_general | solution.py:68
  195.3 0.7 multiply_reduce_fusion
  196.0 1.3 copy-done.5
  197.2 71.1 %all-gather.1 = f32[256,1,256]{2,1,0:T(1,128)S(1)} all-gather(f32[1,1,256]{2,1,0:T(1,128)S(1)} %bitcast.172), channel_id=2, replica_groups=mesh['scene'=16,'seq'=16] {'scene','seq'}, dimensions={0}, use_global_device_ids=true | all-gather | bytes 263168 | tf_op jit(solution)/shard_map/all_gather | solution.py:79
  268.7 0.6 broadcast_multiply_fusion
  269.2 5.1 %fusion.2 = bf16[1,16,256,256]{3,2,1,0:T(8,128)(2,1)} fusion(f32[1,16,256,256]{3,2,1,0:T(8,128)} %copy-done.5, bf16[16,16,256,1]{2,1,0,3:T(8,128)(2,1)S(1)} %bitcast.159, bf16[16,1,1,16,16,256]{5,4,3,2,1,0:T(8,128)(2,1)} %get-tuple-element.14, f32[256]{0:T(256)S(1)} %copy-done.11), kind=kOutput, calls=%fused_computation.7 | convolution fusion | flops 540016640 | bytes 8520704 | tf_op jit(solution)/shard_map/Jjb,Jsajc->sabc/dot_general | solution.py:74
  (24 shorter events, 0.4 us)
Async XLA Ops:
  7.2 1.1 copy-start
  8.2 2.5 copy-start.2
  8.2 2.8 %copy-start.7 = (bf16[1,4096,256]{2,1,0:T(8,128)(2,1)S(1)}, bf16[1,4096,256]{2,1,0:T(8,128)(2,1)}, u32[]{:S(2)}) copy-start(bf16[1,4096,256]{2,1,0:T(8,128)(2,1)} %param.9) | copy-start | bytes 6291460
  8.3 2.8 %copy-start.11 = (f32[256]{0:T(256)S(1)}, f32[256]{0:T(256)}, u32[]{:S(2)}) copy-start(f32[256]{0:T(256)} %param.10) | copy-start | bytes 3076
  16.1 7.6 %copy-start.6 = (bf16[256,16,256]{2,1,0:T(8,128)(2,1)S(1)}, bf16[256,16,256]{2,1,0:T(8,128)(2,1)}, u32[]{:S(2)}) copy-start(bf16[256,16,256]{2,1,0:T(8,128)(2,1)} %param.11) | copy-start | bytes 6291460
  16.1 61.2 %all-to-all-start = ((bf16[16,2,1,16,16,256]{5,4,3,2,1,0:T(8,128)(2,1)}), bf16[16,2,1,16,16,256]{5,4,3,2,1,0:T(8,128)(2,1)}, u32[]{:S(2)}, u32[]{:S(2)}) async-start(bf16[16,2,1,16,16,256]{5,4,3,2,1,0:T(8,128)(2,1)} %copy.34), calls=%async_computation | async-start | bytes 8388608 | tf_op jit(solution)/shard_map/all_to_all | solution.py:33
  80.0 0.9 copy-start.9
  80.9 1.7 copy-start.10
  82.6 1.7 copy-start.4
  84.3 1.9 copy-start.1
  91.7 95.9 %all-to-all-start.1 = ((bf16[16,1,2,16,16,256]{5,4,3,2,1,0:T(8,128)(2,1)}), bf16[16,1,2,16,16,256]{5,4,3,2,1,0:T(8,128)(2,1)}, u32[]{:S(2)}, u32[]{:S(2)}) async-start(bf16[16,1,2,16,16,256]{5,4,3,2,1,0:T(8,128)(2,1)} %maximum_bitcast_fusion), calls=%async_computation.1 | async-start | bytes 8388608 | tf_op jit(solution)/shard_map/all_to_all | solution.py:67
  103.7 170.6 %reduce-scatter.2.cloned.1.call-start = ((), (), s32[]{:S(2)}) async-start(), calls=%async_computation.3 | async-start | bytes 4456448 | tf_op jit(solution)/shard_map/reduce_scatter | solution.py:54
  113.8 77.8 %copy-start.3 = (bf16[1,4096,256]{2,1,0:T(8,128)(2,1)S(1)}, bf16[1,4096,256]{2,1,0:T(8,128)(2,1)}, u32[]{:S(2)}) copy-start(bf16[1,4096,256]{2,1,0:T(8,128)(2,1)} %param.8) | copy-start | bytes 6291460
  187.6 4.1 %copy-start.8 = (bf16[1,4096,256]{2,1,0:T(8,128)(2,1)S(1)}, bf16[1,4096,256]{2,1,0:T(8,128)(2,1)}, u32[]{:S(2)}) copy-start(bf16[1,4096,256]{2,1,0:T(8,128)(2,1)} %param.9) | copy-start | bytes 6291460
  195.3 2.0 copy-start.5
Sparse Core Ops, SparseCore 0:
  114.0 102.4 reduce-scatter.1
